TPU v7x, 256 devices: a whole 4x4x8 slice. The times are simulated.
256 devices in a mesh: seq: 64 (over z, y, core), mp: 4 (over x).
Axes of the slice: x: 4, y: 4, z: 8, core: 2. Of those that a mesh axis runs over, the one named last changes fastest.
Arguments:
- patches: bfloat16 [262144, 1280], P('seq'), may hold values from -2 to 2
- w_qkv: bfloat16 [1280, 3840], P('seq', 'mp'), as said below
- w_out: bfloat16 [1280, 1280], P('mp', 'seq'), may hold values from -0.15625 to 0.15625
- page_rows: int32 [64], replicated, may hold values from 32 to 64, as said below
- page_cols: int32 [64], replicated, may hold values from 32 to 64, as said below
- window_slot: int32 [64, 64], replicated, may hold values from 0 to 63, each once within a row
Outputs:
- blocks: bfloat16 [262144, 1280], P('seq', 'mp')
Inputs may be any that keep to these rules, and one draw needn't show every extreme that they name: `page_rows`: page heights, multiples of 16; some page has the largest. `page_cols`: page widths, multiples of 16; some page has the largest. `window_slot`: each row is a permutation. `w_qkv`: entries of order at most 5.5 / sqrt(1280).
All inputs are finite; a program needn't handle non-finite values.
Results may differ from a plain program's by a relative error of at most 0.012.
Values may be sent and summed in bfloat16 or wider, within the bound.
No kernel may reach another device: no remote copies, remote signals or barrier semaphores. Data moves between devices by JAX's collectives and lax.ppermute only.
A program may use at most 192 MiB of HBM per device.

v0:
```python
import jax
import jax.numpy as jnp
from jax import lax
from jax.sharding import PartitionSpec as P

HD = 80
WS = 8
QUARTERS = 4
EPSILON = 1e-06


def angle_tables(row_place, column_place, head_size):
    quarter = head_size // 4
    frequency = 1.0 / 10000.0 ** (jnp.arange(quarter, dtype=jnp.float32) * 2.0 / (head_size // 2))
    angles = jnp.concatenate(
        [
            row_place[..., None].astype(jnp.float32) * frequency,
            column_place[..., None].astype(jnp.float32) * frequency,
        ],
        axis=-1,
    )
    angles = jnp.concatenate([angles, angles], axis=-1)
    return (jnp.cos(angles), jnp.sin(angles))


def slot_positions(page_widths, slot_table, slot_numbers, window_side):
    matches = slot_table[:, :, None] == slot_numbers[None, None, :]
    ordinal = jnp.arange(slot_table.shape[1], dtype=jnp.int32)
    window = jnp.sum(jnp.where(matches, ordinal[None, :, None], 0), axis=1)
    across = page_widths // window_side
    window_row = window // across[:, None]
    window_column = window % across[:, None]
    unit_side = window_side // 2
    position = jnp.arange(window_side * window_side, dtype=jnp.int32)
    merge_unit = position // 4
    corner = position % 4
    inner_row = merge_unit // unit_side * 2 + corner // 2
    inner_column = merge_unit % unit_side * 2 + corner % 2
    row_place = window_row[:, :, None] * window_side + inner_row
    column_place = window_column[:, :, None] * window_side + inner_column
    return (row_place, column_place)


def block_sources(height, page_width, slot_row, block_count):
    across = page_width // WS
    block = jnp.arange(block_count, dtype=jnp.int32)
    band = block // across
    column = block % across
    window_row = band // QUARTERS
    quarter = band % QUARTERS
    live = window_row < height // WS
    window = jnp.where(live, window_row * across + column, 0)
    ordinal = jnp.arange(slot_row.shape[0], dtype=jnp.int32)
    slot = jnp.sum(jnp.where(window[:, None] == ordinal[None, :], slot_row[None, :], 0), axis=1)
    return (slot * QUARTERS + quarter, live)


def normalize(block_in):
    values = block_in.astype(jnp.float32)
    factor = lax.rsqrt(jnp.mean(values * values, axis=-1, keepdims=True) + EPSILON)
    return (values * factor).astype(jnp.bfloat16)


def rotated_columns(weight):
    half = weight.shape[-1] // 2
    return jnp.concatenate([-weight[..., half:], weight[..., :half]], axis=-1)


def local(patches, w_qkv, w_out, page_rows, page_cols, window_slot):
    seq_index = lax.axis_index("seq")
    seq_count = lax.axis_size("seq")
    mp_index = lax.axis_index("mp")
    page_count = window_slot.shape[0]
    slot_count = window_slot.shape[1]
    slots_held = slot_count // seq_count
    window_tokens = WS * WS
    quarter_tokens = window_tokens // QUARTERS
    model_width = patches.shape[1]
    windows = patches.shape[0] // window_tokens
    own_rows = w_qkv.shape[0]
    heads = w_qkv.shape[1] // (3 * HD)
    qkv = w_qkv.reshape(own_rows, heads, 3, HD)
    w_q = qkv[:, :, 0]
    w_k = qkv[:, :, 1]
    fused_rows = jnp.concatenate(
        [
            w_q.reshape(own_rows, heads * HD),
            w_k.reshape(own_rows, heads * HD),
            rotated_columns(w_q).reshape(own_rows, heads * HD),
            rotated_columns(w_k).reshape(own_rows, heads * HD),
            qkv[:, :, 2].reshape(own_rows, heads * HD),
            w_out.T,
        ],
        axis=1,
    )
    joined = lax.all_gather(fused_rows, "seq", axis=0, tiled=True)
    fused = joined[:, : 5 * heads * HD]
    out_rows_t = joined[:, 5 * heads * HD :]
    out_full_t = lax.all_gather(out_rows_t, "mp", axis=1, tiled=True)
    slot_numbers = seq_index * slots_held + jnp.arange(slots_held, dtype=jnp.int32)
    row_place, column_place = slot_positions(page_cols, window_slot, slot_numbers, WS)
    cosine, sine = angle_tables(
        row_place.reshape(-1, window_tokens), column_place.reshape(-1, window_tokens), HD
    )
    cosine = jnp.tile(cosine.reshape(-1, HD), (1, 2 * heads))
    sine = jnp.tile(sine.reshape(-1, HD), (1, 2 * heads))
    normed = normalize(patches)
    projected = jnp.dot(normed, fused, preferred_element_type=jnp.float32)
    width = heads * HD
    turned = projected[:, : 2 * width] * cosine + projected[:, 2 * width : 4 * width] * sine
    turned = turned.astype(jnp.bfloat16).reshape(windows, window_tokens, 2 * width)
    queries = turned[:, :, :width]
    key_block = turned[:, :, width:]
    values = projected[:, 4 * width :].astype(jnp.bfloat16).reshape(windows, window_tokens, width)
    lane_head = jnp.arange(width, dtype=jnp.int32) // HD
    scale = 1.0 / HD**0.5
    mixed = jnp.zeros((windows, window_tokens, width), jnp.float32)
    for head in range(heads):
        mask = lane_head == head
        picked = jnp.where(mask, queries, jnp.zeros_like(queries))
        scores = (
            jnp.einsum("wqd,wkd->wqk", picked, key_block, preferred_element_type=jnp.float32)
            * scale
        )
        row_max = jnp.max(scores, axis=-1, keepdims=True)
        lifted = jnp.exp(scores - row_max)
        weights = (lifted / jnp.sum(lifted, axis=-1, keepdims=True)).astype(jnp.bfloat16)
        own_values = jnp.where(mask, values, jnp.zeros_like(values))
        mixed = mixed + jnp.einsum(
            "wqk,wkd->wqd", weights, own_values, preferred_element_type=jnp.float32
        )
    mixed = mixed.astype(jnp.bfloat16)
    spread = mixed.reshape(windows, QUARTERS, quarter_tokens, width)
    gathered = lax.all_to_all(spread, "mp", split_axis=1, concat_axis=1, tiled=True)
    out_grouped = out_full_t.reshape(model_width, QUARTERS, width)
    branch = lax.dot_general(
        gathered, out_grouped, (((1, 3), (1, 2)), ((), ())), preferred_element_type=jnp.float32
    )
    branch = branch.reshape(windows * quarter_tokens, model_width)
    residual = patches.reshape(windows, QUARTERS, quarter_tokens, model_width)
    residual = lax.dynamic_index_in_dim(residual, mp_index, 1, keepdims=False)
    residual = residual.reshape(windows * quarter_tokens, model_width).astype(jnp.float32)
    block_out = (residual + branch).astype(jnp.bfloat16)
    share_width = model_width // QUARTERS
    sectioned = block_out.reshape(page_count, quarter_tokens, QUARTERS, share_width)
    sectioned = jnp.transpose(sectioned, (0, 2, 1, 3)).reshape(
        page_count * QUARTERS, quarter_tokens, share_width
    )
    landed = lax.all_to_all(sectioned, ("seq", "mp"), split_axis=0, concat_axis=0, tiled=True)
    own_pages = page_count // seq_count
    first_page = seq_index * own_pages
    heights = lax.dynamic_slice_in_dim(page_rows, first_page, own_pages, 0)
    widths = lax.dynamic_slice_in_dim(page_cols, first_page, own_pages, 0)
    slot_rows = lax.dynamic_slice_in_dim(window_slot, first_page, own_pages, 0)
    block_count = slot_count * QUARTERS // own_pages
    landed = landed.reshape(own_pages, block_count, quarter_tokens, share_width)

    def regroup(received, height, page_width, slot_row):
        source, live = block_sources(height, page_width, slot_row, block_count)
        picked = jnp.take(received, source, axis=0)
        return jnp.where(live[:, None, None], picked, jnp.zeros_like(picked))

    merged = jax.vmap(regroup)(landed, heights, widths, slot_rows)
    return merged.reshape(-1, share_width)


def solution(mesh):
    return jax.shard_map(
        local,
        mesh=mesh,
        in_specs=(P("seq", None), P("seq", "mp"), P("mp", "seq"), P(), P(), P()),
        out_specs=P("seq", "mp"),
        check_vma=False,
    )
```

profile of v0, /device:TPU:1, one launch (start us, length us, event | category | flops | bytes accessed | tf_op | source)
XLA Modules:
  0.0 355.9 jit_solution(10992189034661572990)
XLA Ops:
  8.7 1.5 concatenate.24
  12.5 6.1 %fusion.4 = f32[4096]{0:T(1024)S(1)} fusion(bf16[4096,1280]{1,0:T(8,128)(2,1)} %param.6), kind=kLoop, calls=%fused_computation.7 | loop fusion | flops 15724544 | bytes 10502144 | tf_op jit(solution)/shard_map/reduce_sum | solution.py:60
  18.7 4.8 %fusion.69 = (f32[4096,80]{0,1:T(8,128)S(1)}, f32[4096,80]{0,1:T(8,128)S(1)}) fusion(f32[4096,20]{0,1:T(8,128)S(1)} %get-tuple-element.19, f32[4096,20]{0,1:T(8,128)S(1)} %get-tuple-element.18), kind=kLoop, calls=%fused_computation.88 | loop fusion | flops 983040 | bytes 3276800 | tf_op jit(solution)/shard_map/cos | solution.py:23
  23.5 71.3 %all-gather.6.cloned.1.call-done = bf16[64,20,1920]{2,1,0:T(8,128)(2,1)} async-done(((bf16[1,20,1920]{2,1,0:T(8,128)(2,1)}), bf16[64,20,1920]{2,1,0:T(8,128)(2,1)}) %all-gather.6.cloned.1.call-update) | async-done | bytes 4915216 | tf_op jit(solution)/shard_map/all_gather | solution.py:96
  94.8 7.5 %reshape.662 = bf16[1280,1920]{1,0:T(8,128)(2,1)} reshape(bf16[64,20,1920]{2,1,0:T(8,128)(2,1)} %all-gather.6.cloned.1.call-done) | data formatting | bytes 9830400
  102.3 2.6 slice.72
  104.9 2.2 copy.67
  107.2 23.8 %fusion.6 = f32[4096,1600]{0,1:T(8,128)} fusion(bf16[4096,1280]{1,0:T(8,128)(2,1)} %param.6, f32[4096]{0:T(1024)S(1)} %add_rsqrt_fusion, bf16[1280,1920]{1,0:T(8,128)(2,1)} %reshape.662), kind=kOutput, calls=%fused_computation.9 | convolution fusion | flops 16792944640 | bytes 40976384 | tf_op jit(solution)/shard_map/dot_general | solution.py:108
  131.0 4.4 %slice.125 = bf16[4096,320]{0,1:T(8,128)(2,1)} slice(f32[4096,1600]{0,1:T(8,128)} %fusion.6), slice={[0:4096], [1280:1600]} | slice | bytes 5242880 | tf_op jit(solution)/shard_map/slice | solution.py:114
  135.4 10.4 %fusion.9 = bf16[4096,640]{0,1:T(8,128)(2,1)} fusion(f32[4096,1600]{0,1:T(8,128)} %fusion.6, f32[4096,80]{0,1:T(8,128)S(1)} %get-tuple-element.11, f32[4096,80]{0,1:T(8,128)S(1)} %get-tuple-element.10), kind=kLoop, calls=%fused_computation.12 | loop fusion | flops 10485760 | bytes 28835840 | tf_op jit(solution)/shard_map/convert_element_type | solution.py:111
  145.8 7.9 %copy.60 = bf16[4096,640]{1,0:T(8,128)(2,1)} copy(bf16[4096,640]{0,1:T(8,128)(2,1)} %fusion.9) | data formatting | bytes 10485760 | tf_op jit(solution)/shard_map/convert_element_type | solution.py:111
  153.7 3.5 copy.61
  157.2 5.4 %fusion.20 = f32[64,64,64]{1,2,0:T(8,128)S(1)} fusion(pred[320]{0:T(512)(128)(4,1)S(1)} %broadcast_compare_fusion.1, bf16[64,64,640]{2,1,0:T(8,128)(2,1)} %bitcast.54), kind=kOutput, calls=%fused_computation.28 | convolution fusion | flops 169082880 | bytes 7340352 | tf_op jit(solution)/shard_map/wqd,wkd->wqk/dot_general | solution.py:122
  164.0 1.4 fusion.16
  165.4 1.4 fusion.28
  166.7 1.4 fusion.24
  170.1 5.4 %fusion.22 = f32[64,64,320]{2,1,0:T(8,128)} fusion(bf16[64,64,320]{2,1,0:T(8,128)(2,1)S(1)} %bitcast.50, pred[320]{0:T(512)(128)(4,1)S(1)} %broadcast_compare_fusion.3, f32[64,64]{1,0:T(8,128)S(1)} %fusion.127, f32[64,64,64]{1,2,0:T(8,128)} %copy-done.7), kind=kOutput, calls=%fused_computation.30 | convolution fusion | flops 170135616 | bytes 8929600 | tf_op jit(solution)/shard_map/wqk,wkd->wqd/dot_general | solution.py:129
  175.5 5.4 %fusion.14 = f32[64,64,320]{2,1,0:T(8,128)} fusion(bf16[64,64,320]{2,1,0:T(8,128)(2,1)S(1)} %bitcast.51, pred[320]{0:T(512)(128)(4,1)S(1)} %broadcast_compare_fusion, f32[64,64]{1,0:T(8,128)S(1)} %fusion.125, f32[64,64,64]{1,2,0:T(8,128)} %copy-done.6), kind=kOutput, calls=%fused_computation.22 | convolution fusion | flops 170135616 | bytes 8929600 | tf_op jit(solution)/shard_map/wqk,wkd->wqd/dot_general | solution.py:129
  180.9 5.3 %fusion.18 = f32[64,64,320]{2,1,0:T(8,128)} fusion(bf16[64,64,320]{2,1,0:T(8,128)(2,1)S(1)} %bitcast.52, pred[320]{0:T(512)(128)(4,1)S(1)} %broadcast_compare_fusion.1, f32[64,64]{1,0:T(8,128)S(1)} %fusion.126, f32[64,64,64]{1,2,0:T(8,128)} %copy-done.5), kind=kOutput, calls=%fused_computation.26 | convolution fusion | flops 170135616 | bytes 8929600 | tf_op jit(solution)/shard_map/wqk,wkd->wqd/dot_general | solution.py:129
  186.2 9.9 %add_convert_fusion = bf16[64,64,320]{2,1,0:T(8,128)(2,1)S(1)} fusion(f32[64,64,320]{2,1,0:T(8,128)} %fusion.14, f32[64,64,320]{2,1,0:T(8,128)} %fusion.18, f32[64,64,320]{2,1,0:T(8,128)} %fusion.22, bf16[64,64,320]{2,1,0:T(8,128)(2,1)} %bitcast.53, pred[320]{0:T(512)(128)(4,1)S(1)} %broadcast_compare_fusion.2, f32[64,64]{1,0:T(8,128)S(1)} %fusion.128, ...), kind=kOutput, calls=%fused_computation.15 | convolution fusion | flops 175378496 | bytes 22036800 | tf_op jit(solution)/shard_map/wqk,wkd->wqd/dot_general | solution.py:129
  196.1 2.0 copy.66
  198.1 3.9 %all-to-all-start = ((bf16[64,4,16,320]{3,2,0,1:T(8,128)(2,1)}), bf16[64,4,16,320]{3,2,0,1:T(8,128)(2,1)S(1)}, u32[]{:S(2)}, u32[]{:S(2)}) async-start(bf16[64,4,16,320]{3,2,0,1:T(8,128)(2,1)} %copy.66), calls=%async_computation | async-start | bytes 6291456 | tf_op jit(solution)/shard_map/all_to_all | solution.py:134
  201.9 3.4 constant_dynamic-slice_fusion
  205.4 33.7 %all-to-all-done = bf16[64,4,16,320]{3,2,0,1:T(8,128)(2,1)S(1)} async-done(((bf16[64,4,16,320]{3,2,0,1:T(8,128)(2,1)}), bf16[64,4,16,320]{3,2,0,1:T(8,128)(2,1)S(1)}, u32[]{:S(2)}, u32[]{:S(2)}) %all-to-all-start) | async-done | bytes 2621472 | tf_op jit(solution)/shard_map/all_to_all | solution.py:134
  239.0 7.3 %fusion.11 = bf16[1024,1280]{1,0:T(8,128)(2,1)} fusion(bf16[1024,1280]{1,0:T(8,128)(2,1)} %bitcast.59, bf16[1024,4,320]{2,0,1:T(8,128)(2,1)S(1)} %bitcast.58, bf16[1280,4,320]{0,2,1:T(8,128)(2,1)} %bitcast.63), kind=kOutput, calls=%fused_computation.18 | convolution fusion | flops 3359375360 | bytes 11141120 | tf_op jit(solution)/shard_map/dot_general | solution.py:136
  246.3 6.1 %reshape.648 = bf16[64,16,4,320]{3,2,1,0:T(4,128)(2,1)S(1)} reshape(bf16[1024,1280]{1,0:T(8,128)(2,1)} %fusion.11) | data formatting | bytes 5242880 | tf_op jit(solution)/shard_map/reshape | solution.py:145
  252.4 2.4 copy.69
  254.8 7.8 %all-to-all-start.1 = ((bf16[256,16,320]{2,1,0:T(8,128)(2,1)}), bf16[256,16,320]{2,1,0:T(8,128)(2,1)S(1)}, u32[]{:S(2)}, u32[]{:S(2)}) async-start(bf16[256,16,320]{2,1,0:T(8,128)(2,1)} %bitcast.48), calls=%async_computation.1 | async-start | bytes 6291456 | tf_op jit(solution)/shard_map/all_to_all | solution.py:149
  270.6 67.9 %all-to-all-done.1 = bf16[256,16,320]{2,1,0:T(8,128)(2,1)S(1)} async-done(((bf16[256,16,320]{2,1,0:T(8,128)(2,1)}), bf16[256,16,320]{2,1,0:T(8,128)(2,1)S(1)}, u32[]{:S(2)}, u32[]{:S(2)}) %all-to-all-start.1) | async-done | bytes 2621472 | tf_op jit(solution)/shard_map/all_to_all | solution.py:149
  338.6 2.7 gather_fusion
  341.3 5.0 %fusion.13 = bf16[4096,320]{1,0:T(8,128)(2,1)S(1)} fusion(bf16[256,16,320]{2,1,0:T(8,128)(2,1)} %gather_fusion, pred[4096]{0:T(1024)(128)(4,1)S(1)} %broadcast_in_dim.141, pred[4096]{0:T(1024)(128)(4,1)S(1)} %broadcast_in_dim.135), kind=kLoop, calls=%fused_computation.21 | loop fusion | flops 2621440 | bytes 5251072 | tf_op jit(solution)/shard_map/vmap(jit(_where))/select_n | solution.py:161
  346.3 2.7 copy.70
  (66 shorter events, 10.7 us)
Async XLA Ops:
  6.5 88.3 %all-gather.6.cloned.1.call-start = ((), (), s32[]{:S(2)}) async-start(), calls=%async_computation.3 | async-start | bytes 5990400 | tf_op jit(solution)/shard_map/all_gather | solution.py:96
  10.2 228.8 %all-gather.4.cloned.1.call-start = ((), (), s32[]{:S(2)}) async-start(), calls=%async_computation.2 | async-start | bytes 4096000 | tf_op jit(solution)/shard_map/all_gather | solution.py:99
  157.2 23.6 %copy-start = (bf16[4096,320]{1,0:T(8,128)(2,1)}, bf16[4096,320]{1,0:T(8,128)(2,1)S(1)}, u32[]{:S(2)}) copy-start(bf16[4096,320]{1,0:T(8,128)(2,1)S(1)} %copy.61) | copy-start | bytes 7864324
  157.2 6.7 %copy-start.1 = (bf16[4096,640]{1,0:T(8,128)(2,1)S(1)}, bf16[4096,640]{1,0:T(8,128)(2,1)}, u32[]{:S(2)}) copy-start(bf16[4096,640]{1,0:T(8,128)(2,1)} %copy.60) | copy-start | bytes 15728644
  162.6 1.4 copy-start.5
  165.3 2.8 copy-start.6
  166.7 2.7 copy-start.2
  168.1 2.0 copy-start.7
  198.1 41.0 %all-to-all-start = ((bf16[64,4,16,320]{3,2,0,1:T(8,128)(2,1)}), bf16[64,4,16,320]{3,2,0,1:T(8,128)(2,1)S(1)}, u32[]{:S(2)}, u32[]{:S(2)}) async-start(bf16[64,4,16,320]{3,2,0,1:T(8,128)(2,1)} %copy.66), calls=%async_computation | async-start | bytes 6291456 | tf_op jit(solution)/shard_map/all_to_all | solution.py:134
  254.8 7.8 %copy-start.3 = (s32[64]{0:T(128)S(1)}, s32[64]{0:T(128)}, u32[]{:S(2)}) copy-start(s32[64]{0:T(128)} %param.10) | copy-start | bytes 772
  254.8 11.0 %copy-start.4 = (s32[64]{0:T(128)S(1)}, s32[64]{0:T(128)}, u32[]{:S(2)}) copy-start(s32[64]{0:T(128)} %param.9) | copy-start | bytes 772
  254.8 83.8 %all-to-all-start.1 = ((bf16[256,16,320]{2,1,0:T(8,128)(2,1)}), bf16[256,16,320]{2,1,0:T(8,128)(2,1)S(1)}, u32[]{:S(2)}, u32[]{:S(2)}) async-start(bf16[256,16,320]{2,1,0:T(8,128)(2,1)} %bitcast.48), calls=%async_computation.1 | async-start | bytes 6291456 | tf_op jit(solution)/shard_map/all_to_all | solution.py:149
Sparse Core Ops, SparseCore 0:
  10.4 84.3 all-gather.5
  107.3 39.4 all-gather.3
where the time goes:
time: 357 us; the launch traced here: 356 us
  waiting for transfers between devices  173 us (48%)
  matrix products  66.5 us (19%)
  local copies, waits for them, and re-layouts  54 us (15%)
  other arithmetic  31.8 us (9%)
  between operations  18.9 us (5%)
  starting transfers between devices  11.7 us (3%)
    all_gather x1, waiting for transfers between devices, local(): joined = lax.all_gather(fused_rows, 'seq', axis=0, tiled=True)  71.3 us
    all_to_all x1, waiting for transfers between devices, local(): lax.all_to_all(sectioned, ('seq', 'mp'), split_axis=0, concat_axis=0, til...  67.9 us
    all_to_all x1, waiting for transfers between devices, local(): lax.all_to_all(spread, 'mp', split_axis=1, concat_axis=1, tiled=True)  33.7 us
    dot_general x4, matrix products, local(): jnp.einsum('wqk,wkd->wqd', weights, own_values, preferred_element_type=jn...  26 us
    dot_general x1, matrix products, local(): projected = jnp.dot(normed, fused, preferred_element_type=jnp.float32)  23.8 us
    convert_element_type x1, other arithmetic, local(): turned.astype(jnp.bfloat16).reshape(windows, window_tokens, 2 * width)  10.4 us
    dot_general x4, matrix products, local(): jnp.einsum('wqd,wkd->wqk', picked, key_block, preferred_element_type=jnp....  9.45 us
    reshape x2, local copies, waits for them, and re-layouts, local(): block_out.reshape(page_count, quarter_tokens, QUARTERS, share_width)  8.5 us
  transfers between devices with their start and end apart: 4, of which 3 were waited for; matrix products, arithmetic and copies ran while one was open for 31% of the time, Pallas kernels for 0%

commit v1 on v0

--- a/solution.py
+++ b/solution.py
@@ -67,6 +67,13 @@
 
 
 def local(patches, w_qkv, w_out, page_rows, page_cols, window_slot):
+
+    def arrange_blocks(sheet):
+        return jnp.concatenate(
+            lax.all_to_all(jnp.stack(jnp.split(sheet, lax.axis_size("mp"), axis=1)), "mp", 0, 0),
+            axis=1,
+        )
+
     seq_index = lax.axis_index("seq")
     seq_count = lax.axis_size("seq")
     mp_index = lax.axis_index("mp")
@@ -131,7 +138,7 @@
         )
     mixed = mixed.astype(jnp.bfloat16)
     spread = mixed.reshape(windows, QUARTERS, quarter_tokens, width)
-    gathered = lax.all_to_all(spread, "mp", split_axis=1, concat_axis=1, tiled=True)
+    gathered = arrange_blocks(spread)
     out_grouped = out_full_t.reshape(model_width, QUARTERS, width)
     branch = lax.dot_general(
         gathered, out_grouped, (((1, 3), (1, 2)), ((), ())), preferred_element_type=jnp.float32

time: 357 us -> 357 us (level)
  no operation moved by 1% of the time
where the time goes in v1:
time: 357 us; the launch traced here: 356 us
  waiting for transfers between devices  173 us (48%)
  matrix products  66.5 us (19%)
  local copies, waits for them, and re-layouts  51.6 us (14%)
  other arithmetic  33.9 us (9%)
  between operations  18.9 us (5%)
  starting transfers between devices  11.8 us (3%)
    all_gather x1, waiting for transfers between devices, local(): joined = lax.all_gather(fused_rows, 'seq', axis=0, tiled=True)  71.3 us
    all_to_all x1, waiting for transfers between devices, local(): lax.all_to_all(sectioned, ('seq', 'mp'), split_axis=0, concat_axis=0, til...  67.9 us
    all_to_all x1, waiting for transfers between devices, arrange_blocks(): lax.all_to_all(jnp.stack(jnp.split(sheet, lax.axis_size('mp'), axis=1)),...  33.7 us
    dot_general x4, matrix products, local(): jnp.einsum('wqk,wkd->wqd', weights, own_values, preferred_element_type=jn...  26 us
    dot_general x1, matrix products, local(): projected = jnp.dot(normed, fused, preferred_element_type=jnp.float32)  23.8 us
    convert_element_type x1, other arithmetic, local(): turned.astype(jnp.bfloat16).reshape(windows, window_tokens, 2 * width)  10.4 us
    dot_general x4, matrix products, local(): jnp.einsum('wqd,wkd->wqk', picked, key_block, preferred_element_type=jnp....  9.44 us
    reshape x2, local copies, waits for them, and re-layouts, local(): block_out.reshape(page_count, quarter_tokens, QUARTERS, share_width)  8.5 us
  transfers between devices with their start and end apart: 4, of which 3 were waited for; matrix products, arithmetic and copies ran while one was open for 31% of the time, Pallas kernels for 0%

profile of v1, /device:TPU:1, one launch (start us, length us, event | category | flops | bytes accessed | tf_op | source)
XLA Modules:
  0.0 355.6 jit_solution(4224788765711841023)
XLA Ops:
  8.7 1.5 concatenate.24
  12.5 6.1 %fusion.4 = f32[4096]{0:T(1024)S(1)} fusion(bf16[4096,1280]{1,0:T(8,128)(2,1)} %param.6), kind=kLoop, calls=%fused_computation.7 | loop fusion | flops 15724544 | bytes 10502144 | tf_op jit(solution)/shard_map/reduce_sum | solution.py:60
  18.7 4.8 %fusion.69 = (f32[4096,80]{0,1:T(8,128)S(1)}, f32[4096,80]{0,1:T(8,128)S(1)}) fusion(f32[4096,20]{0,1:T(8,128)S(1)} %get-tuple-element.23, f32[4096,20]{0,1:T(8,128)S(1)} %get-tuple-element.22), kind=kLoop, calls=%fused_computation.89 | loop fusion | flops 983040 | bytes 3276800 | tf_op jit(solution)/shard_map/cos | solution.py:23
  23.5 71.3 %all-gather.6.cloned.1.call-done = bf16[64,20,1920]{2,1,0:T(8,128)(2,1)} async-done(((bf16[1,20,1920]{2,1,0:T(8,128)(2,1)}), bf16[64,20,1920]{2,1,0:T(8,128)(2,1)}) %all-gather.6.cloned.1.call-update) | async-done | bytes 4915216 | tf_op jit(solution)/shard_map/all_gather | solution.py:103
  94.8 7.5 %reshape.670 = bf16[1280,1920]{1,0:T(8,128)(2,1)} reshape(bf16[64,20,1920]{2,1,0:T(8,128)(2,1)} %all-gather.6.cloned.1.call-done) | data formatting | bytes 9830400
  102.3 2.6 slice.72
  104.9 2.2 copy.82
  107.2 23.8 %fusion.6 = f32[4096,1600]{0,1:T(8,128)} fusion(bf16[4096,1280]{1,0:T(8,128)(2,1)} %param.6, f32[4096]{0:T(1024)S(1)} %add_rsqrt_fusion, bf16[1280,1920]{1,0:T(8,128)(2,1)} %reshape.670), kind=kOutput, calls=%fused_computation.9 | convolution fusion | flops 16792944640 | bytes 40976384 | tf_op jit(solution)/shard_map/dot_general | solution.py:115
  131.0 4.4 %slice.125 = bf16[4096,320]{0,1:T(8,128)(2,1)} slice(f32[4096,1600]{0,1:T(8,128)} %fusion.6), slice={[0:4096], [1280:1600]} | slice | bytes 5242880 | tf_op jit(solution)/shard_map/slice | solution.py:121
  135.4 10.4 %fusion.9 = bf16[4096,640]{0,1:T(8,128)(2,1)} fusion(f32[4096,1600]{0,1:T(8,128)} %fusion.6, f32[4096,80]{0,1:T(8,128)S(1)} %get-tuple-element.15, f32[4096,80]{0,1:T(8,128)S(1)} %get-tuple-element.14), kind=kLoop, calls=%fused_computation.12 | loop fusion | flops 10485760 | bytes 28835840 | tf_op jit(solution)/shard_map/convert_element_type | solution.py:118
  145.8 7.9 %copy.72 = bf16[4096,640]{1,0:T(8,128)(2,1)} copy(bf16[4096,640]{0,1:T(8,128)(2,1)} %fusion.9) | data formatting | bytes 10485760 | tf_op jit(solution)/shard_map/convert_element_type | solution.py:118
  153.7 3.5 copy.73
  157.2 5.4 %fusion.20 = f32[64,64,64]{1,2,0:T(8,128)S(1)} fusion(pred[320]{0:T(512)(128)(4,1)S(1)} %broadcast_compare_fusion.1, bf16[64,64,640]{2,1,0:T(8,128)(2,1)} %bitcast.74), kind=kOutput, calls=%fused_computation.29 | convolution fusion | flops 169082880 | bytes 7340352 | tf_op jit(solution)/shard_map/wqd,wkd->wqk/dot_general | solution.py:129
  163.3 1.4 fusion.16
  165.3 1.4 fusion.28
  166.7 1.4 fusion.24
  169.4 5.4 %fusion.22 = f32[64,64,320]{2,1,0:T(8,128)} fusion(bf16[64,64,320]{2,1,0:T(8,128)(2,1)S(1)} %bitcast.70, pred[320]{0:T(512)(128)(4,1)S(1)} %broadcast_compare_fusion.3, f32[64,64]{1,0:T(8,128)S(1)} %fusion.127, f32[64,64,64]{1,2,0:T(8,128)} %copy-done.7), kind=kOutput, calls=%fused_computation.31 | convolution fusion | flops 170135616 | bytes 8929600 | tf_op jit(solution)/shard_map/wqk,wkd->wqd/dot_general | solution.py:136
  174.8 5.4 %fusion.14 = f32[64,64,320]{2,1,0:T(8,128)} fusion(bf16[64,64,320]{2,1,0:T(8,128)(2,1)S(1)} %bitcast.71, pred[320]{0:T(512)(128)(4,1)S(1)} %broadcast_compare_fusion, f32[64,64]{1,0:T(8,128)S(1)} %fusion.125, f32[64,64,64]{1,2,0:T(8,128)} %copy-done.6), kind=kOutput, calls=%fused_computation.23 | convolution fusion | flops 170135616 | bytes 8929600 | tf_op jit(solution)/shard_map/wqk,wkd->wqd/dot_general | solution.py:136
  180.2 5.3 %fusion.18 = f32[64,64,320]{2,1,0:T(8,128)} fusion(bf16[64,64,320]{2,1,0:T(8,128)(2,1)S(1)} %bitcast.72, pred[320]{0:T(512)(128)(4,1)S(1)} %broadcast_compare_fusion.1, f32[64,64]{1,0:T(8,128)S(1)} %fusion.126, f32[64,64,64]{1,2,0:T(8,128)} %copy-done.5), kind=kOutput, calls=%fused_computation.27 | convolution fusion | flops 170135616 | bytes 8929600 | tf_op jit(solution)/shard_map/wqk,wkd->wqd/dot_general | solution.py:136
  185.5 9.9 %add_convert_fusion = bf16[64,64,320]{2,1,0:T(8,128)(2,1)S(1)} fusion(f32[64,64,320]{2,1,0:T(8,128)} %fusion.14, f32[64,64,320]{2,1,0:T(8,128)} %fusion.18, f32[64,64,320]{2,1,0:T(8,128)} %fusion.22, bf16[64,64,320]{2,1,0:T(8,128)(2,1)} %bitcast.73, pred[320]{0:T(512)(128)(4,1)S(1)} %broadcast_compare_fusion.2, f32[64,64]{1,0:T(8,128)S(1)} %fusion.128, ...), kind=kOutput, calls=%fused_computation.15 | convolution fusion | flops 175378496 | bytes 22036800 | tf_op jit(solution)/shard_map/wqk,wkd->wqd/dot_general | solution.py:136
  195.7 2.1 pad_maximum_fusion
  197.8 3.9 %all-to-all-start = ((bf16[4,64,1,16,320]{4,3,1,2,0:T(8,128)(2,1)}), bf16[4,64,1,16,320]{4,3,1,2,0:T(8,128)(2,1)S(1)}, u32[]{:S(2)}, u32[]{:S(2)}) async-start(bf16[4,64,1,16,320]{4,3,1,2,0:T(8,128)(2,1)} %pad_maximum_fusion), calls=%async_computation | async-start | bytes 6291456 | tf_op jit(solution)/shard_map/all_to_all | solution.py:73
  201.7 3.4 constant_dynamic-slice_fusion
  205.1 33.7 %all-to-all-done = bf16[4,64,1,16,320]{4,3,1,2,0:T(8,128)(2,1)S(1)} async-done(((bf16[4,64,1,16,320]{4,3,1,2,0:T(8,128)(2,1)}), bf16[4,64,1,16,320]{4,3,1,2,0:T(8,128)(2,1)S(1)}, u32[]{:S(2)}, u32[]{:S(2)}) %all-to-all-start) | async-done | bytes 2621472 | tf_op jit(solution)/shard_map/all_to_all | solution.py:73
  238.7 7.3 %fusion.11 = bf16[1024,1280]{1,0:T(8,128)(2,1)} fusion(bf16[1024,1280]{1,0:T(8,128)(2,1)} %bitcast.79, bf16[1024,4,320]{2,0,1:T(8,128)(2,1)S(1)} %bitcast.78, bf16[1280,4,320]{0,2,1:T(8,128)(2,1)} %bitcast.83), kind=kOutput, calls=%fused_computation.18 | convolution fusion | flops 3359375360 | bytes 11141120 | tf_op jit(solution)/shard_map/dot_general | solution.py:143
  246.0 6.1 %reshape.656 = bf16[64,16,4,320]{3,2,1,0:T(4,128)(2,1)S(1)} reshape(bf16[1024,1280]{1,0:T(8,128)(2,1)} %fusion.11) | data formatting | bytes 5242880 | tf_op jit(solution)/shard_map/reshape | solution.py:152
  252.1 2.4 copy.84
  254.5 7.8 %all-to-all-start.1 = ((bf16[256,16,320]{2,1,0:T(8,128)(2,1)}), bf16[256,16,320]{2,1,0:T(8,128)(2,1)S(1)}, u32[]{:S(2)}, u32[]{:S(2)}) async-start(bf16[256,16,320]{2,1,0:T(8,128)(2,1)} %bitcast.68), calls=%async_computation.1 | async-start | bytes 6291456 | tf_op jit(solution)/shard_map/all_to_all | solution.py:156
  270.4 67.9 %all-to-all-done.1 = bf16[256,16,320]{2,1,0:T(8,128)(2,1)S(1)} async-done(((bf16[256,16,320]{2,1,0:T(8,128)(2,1)}), bf16[256,16,320]{2,1,0:T(8,128)(2,1)S(1)}, u32[]{:S(2)}, u32[]{:S(2)}) %all-to-all-start.1) | async-done | bytes 2621472 | tf_op jit(solution)/shard_map/all_to_all | solution.py:156
  338.3 2.7 gather_fusion
  341.0 5.0 %fusion.13 = bf16[4096,320]{1,0:T(8,128)(2,1)S(1)} fusion(bf16[256,16,320]{2,1,0:T(8,128)(2,1)} %gather_fusion, pred[4096]{0:T(1024)(128)(4,1)S(1)} %broadcast_in_dim.141, pred[4096]{0:T(1024)(128)(4,1)S(1)} %broadcast_in_dim.135), kind=kLoop, calls=%fused_computation.22 | loop fusion | flops 2621440 | bytes 5251072 | tf_op jit(solution)/shard_map/vmap(jit(_where))/select_n | solution.py:168
  346.0 2.7 copy.85
  (67 shorter events, 10.3 us)
Async XLA Ops:
  6.5 88.3 %all-gather.6.cloned.1.call-start = ((), (), s32[]{:S(2)}) async-start(), calls=%async_computation.3 | async-start | bytes 5990400 | tf_op jit(solution)/shard_map/all_gather | solution.py:103
  10.2 228.5 %all-gather.4.cloned.1.call-start = ((), (), s32[]{:S(2)}) async-start(), calls=%async_computation.2 | async-start | bytes 4096000 | tf_op jit(solution)/shard_map/all_gather | solution.py:106
  157.2 22.9 %copy-start = (bf16[4096,320]{1,0:T(8,128)(2,1)}, bf16[4096,320]{1,0:T(8,128)(2,1)S(1)}, u32[]{:S(2)}) copy-start(bf16[4096,320]{1,0:T(8,128)(2,1)S(1)} %copy.73) | copy-start | bytes 7864324
  157.2 6.0 %copy-start.1 = (bf16[4096,640]{1,0:T(8,128)(2,1)S(1)}, bf16[4096,640]{1,0:T(8,128)(2,1)}, u32[]{:S(2)}) copy-start(bf16[4096,640]{1,0:T(8,128)(2,1)} %copy.72) | copy-start | bytes 15728644
  162.6 2.0 copy-start.5
  164.7 2.0 copy-start.6
  166.7 2.0 copy-start.2
  168.1 1.3 copy-start.7
  197.8 41.0 %all-to-all-start = ((bf16[4,64,1,16,320]{4,3,1,2,0:T(8,128)(2,1)}), bf16[4,64,1,16,320]{4,3,1,2,0:T(8,128)(2,1)S(1)}, u32[]{:S(2)}, u32[]{:S(2)}) async-start(bf16[4,64,1,16,320]{4,3,1,2,0:T(8,128)(2,1)} %pad_maximum_fusion), calls=%async_computation | async-start | bytes 6291456 | tf_op jit(solution)/shard_map/all_to_all | solution.py:73
  254.5 7.8 %copy-start.3 = (s32[64]{0:T(128)S(1)}, s32[64]{0:T(128)}, u32[]{:S(2)}) copy-start(s32[64]{0:T(128)} %param.10) | copy-start | bytes 772
  254.5 11.0 %copy-start.4 = (s32[64]{0:T(128)S(1)}, s32[64]{0:T(128)}, u32[]{:S(2)}) copy-start(s32[64]{0:T(128)} %param.9) | copy-start | bytes 772
  254.5 83.8 %all-to-all-start.1 = ((bf16[256,16,320]{2,1,0:T(8,128)(2,1)}), bf16[256,16,320]{2,1,0:T(8,128)(2,1)S(1)}, u32[]{:S(2)}, u32[]{:S(2)}) async-start(bf16[256,16,320]{2,1,0:T(8,128)(2,1)} %bitcast.68), calls=%async_computation.1 | async-start | bytes 6291456 | tf_op jit(solution)/shard_map/all_to_all | solution.py:156
Sparse Core Ops, SparseCore 0:
  10.4 84.3 all-gather.5
  107.3 39.4 all-gather.3
